TPU v7x, 32 devices: a whole 2x2x4 slice. The times are simulated.
32 devices in a mesh: cell: 4 (over y, x), blk: 8 (over z, core).
Axes of the slice: x: 2, y: 2, z: 4, core: 2. Of those that a mesh axis runs over, the one named last changes fastest.
Arguments:
- codes: bfloat16 [16384, 128], P(('cell', 'blk')), may hold values from -60 to 60
- scales: float32 [16384], P(('cell', 'blk')), may hold values from 0.5 to 2
- coarse_ids: int32 [16384], P(('cell', 'blk')), may hold values from 0 to 3, as said below
- centroids: bfloat16 [32768, 128], P(('cell', 'blk')), may hold values from -6 to 6
Outputs:
- reconstruction: bfloat16 [16384, 128], P(('cell', 'blk'))
- residual: bfloat16 [16384, 128], P(('cell', 'blk'))
Inputs may be any that keep to these rules, and one draw needn't show every extreme that they name: `coarse_ids`: on every device, the number of its 512 rows that name partition g is the same for all devices; at most 256 rows of one device name one partition, and one partition is named by exactly 256 rows of every device.
All inputs are finite; a program needn't handle non-finite values.
Results may differ from a plain program's by a relative error of at most 0.006.
Values may be sent and summed in bfloat16 or wider, within the bound.
No kernel may reach another device: no remote copies, remote signals or barrier semaphores. Data moves between devices by JAX's collectives and lax.ppermute only.
A program may use at most 256 MiB of HBM per device.

v0:
```python
import math
import jax
import jax.numpy as jnp
from jax import lax
from jax.sharding import PartitionSpec as P


def local(codes, scales, coarse_ids, centroids):
    rows_dev = codes.shape[0]
    width = codes.shape[1]
    loops = lax.axis_size("cell")
    cap = 2 * rows_dev // loops
    beta = 1.0 / math.sqrt(width)
    dequant = (codes.astype(jnp.float32) * scales[:, None]).astype(jnp.bfloat16)
    onehot = (coarse_ids[:, None] == jnp.arange(loops, dtype=jnp.int32)[None, :]).astype(jnp.int32)
    ranks = jnp.sum(jnp.cumsum(onehot, axis=0) * onehot, axis=1) - 1
    slots = coarse_ids * cap + ranks
    outgoing = jnp.zeros((loops * cap, width), jnp.bfloat16).at[slots].set(dequant)
    arrived = lax.all_to_all(
        outgoing.reshape(loops, cap, width), "cell", split_axis=0, concat_axis=0, tiled=True
    )
    queries = arrived.reshape(loops * cap, width)

    def scores_of(piece):
        product = lax.dot_general(
            queries, piece, (((1,), (1,)), ((), ())), preferred_element_type=jnp.float32
        )
        return product * beta

    top = jnp.max(scores_of(lax.all_gather(centroids, "blk", axis=0, tiled=True)), axis=1)
    piece = lax.all_gather(centroids, "blk", axis=0, tiled=True)
    weights = jnp.exp(scores_of(piece) - top[:, None]).astype(jnp.bfloat16)
    total = jnp.sum(weights.astype(jnp.float32), axis=1)
    numer = jnp.dot(weights, piece, preferred_element_type=jnp.float32)
    total, numer = (total, numer)
    recon = (numer / total[:, None]).astype(jnp.bfloat16)
    remote_residual = (queries.astype(jnp.float32) - recon.astype(jnp.float32)).astype(jnp.bfloat16)
    stacked = jnp.stack([recon, remote_residual]).reshape(2, loops, cap, width)
    back = lax.all_to_all(stacked, "cell", split_axis=1, concat_axis=1, tiled=True).reshape(
        2, loops * cap, width
    )
    return (back[0][slots], back[1][slots])


def solution(mesh):
    in_specs = (
        P(("cell", "blk"), None),
        P(("cell", "blk")),
        P(("cell", "blk")),
        P(("cell", "blk"), None),
    )
    out_specs = (P(("cell", "blk"), None), P(("cell", "blk"), None))
    return jax.shard_map(local, mesh=mesh, in_specs=in_specs, out_specs=out_specs, check_vma=False)
```

profile of v0, /device:TPU:0, one launch (start us, length us, event | category | flops | bytes accessed | tf_op | source)
XLA Modules:
  0.0 99.3 jit_solution(16947095340633523881)
XLA Ops:
  7.2 0.0 all-gather.2.cloned.1.call-start
  7.2 0.7 all-gather.2.cloned.1.call-update
  7.9 0.7 fusion.6
  8.6 1.2 %reduce-window.6 = s32[4,4,128]{2,1,0:T(4,128)S(1)} reduce-window(s32[4,4,128]{2,1,0:T(4,128)S(1)} %fusion.6, s32[]{:T(128)} %constant.4.clone.1), window={size=1x1x128 pad=0_0x0_0x127_0}, to_apply=%region_0.0 | reduce-window | flops 260096 | bytes 16388 | tf_op jit(solution)/shard_map/reduce-window
  9.8 0.2 slice_reduce_fusion
  10.0 0.2 reduce-window.9
  10.2 0.1 add_bitcast_fusion
  10.3 0.7 fusion.5
  11.0 0.7 compare_select_fusion
  11.7 2.3 %scatter_custom_fusion = bf16[1024,128]{1,0:T(8,128)(2,1)S(1)} fusion(s32[512]{0:T(512)S(1)} %compare_select_fusion, bf16[512,128]{1,0:T(8,128)(2,1)} %param.4, f32[512]{0:T(512)} %param.5, bf16[]{:T(256)} %constant.8.clone.1), kind=kCustom, calls=%fused_computation.11 | custom fusion | flops 196608 | bytes 395266 | tf_op jit(solution)/shard_map/scatter | solution.py:18
  14.0 10.7 %all_to_all.10 = bf16[4,256,128]{2,1,0:T(8,128)(2,1)S(1)} all-to-all(bf16[4,256,128]{2,1,0:T(8,128)(2,1)S(1)} %bitcast.34), channel_id=1, replica_groups=mesh['cell'=4,'blk'=8] {'cell'}, dimensions={0} | all-to-all | bytes 524288 | tf_op jit(solution)/shard_map/all_to_all | solution.py:19
  24.7 16.8 %all-gather.2.cloned.1.call-done = bf16[8192,128]{1,0:T(8,128)(2,1)} async-done(((bf16[1024,128]{1,0:T(8,128)(2,1)}), bf16[8192,128]{1,0:T(8,128)(2,1)}) %all-gather.2.cloned.1.call-update) | async-done | bytes 2097168 | tf_op jit(solution)/shard_map/all_gather | solution.py:31
  41.5 14.6 %multiply_reduce_fusion = (f32[1024]{0:T(1024)S(1)}, f32[1024,8192]{1,0:T(8,128)}) fusion(bf16[1024,128]{1,0:T(8,128)(2,1)S(1)} %bitcast.33, bf16[8192,128]{1,0:T(8,128)(2,1)} %all-gather.2.cloned.1.call-done), kind=kOutput, calls=%fused_computation.5 | convolution fusion | flops 2164259840 | bytes 35917824 | tf_op jit(solution)/shard_map/dot_general | solution.py:25
  56.1 0.0 copy-start
  56.1 15.0 %convert_reduce_fusion = (f32[1024]{0:T(1024)S(1)}, bf16[1024,8192]{1,0:T(8,128)(2,1)S(1)}) fusion(f32[1024]{0:T(1024)S(1)} %get-tuple-element.6, f32[1024,8192]{1,0:T(8,128)} %get-tuple-element.7), kind=kLoop, calls=%fused_computation.3 | loop fusion | flops 41942016 | bytes 50339840 | tf_op jit(solution)/shard_map/reduce_sum | solution.py:33
  71.1 0.0 copy-done
  71.1 4.5 %subtract_convert_fusion = (bf16[1024,128]{1,0:T(8,128)(2,1)S(1)}, bf16[1024,128]{1,0:T(8,128)(2,1)S(1)}) fusion(bf16[4,256,128]{2,1,0:T(8,128)(2,1)S(1)} %all_to_all.10, f32[1024]{0:T(1024)S(1)} %get-tuple-element.2, bf16[1024,8192]{1,0:T(8,128)(2,1)S(1)} %get-tuple-element.3, bf16[8192,128]{1,0:T(8,128)(2,1)S(1)} %copy-done), kind=kOutput, calls=%fused_computation.9 | convolution fusion | flops 2148270080 | bytes 19664896 | tf_op jit(solution)/shard_map/dot_general | solution.py:34
  75.6 0.8 pad_maximum_fusion
  76.4 3.6 %all-to-all-start.1 = ((bf16[2,4,256,128]{3,2,0,1:T(8,128)(2,1)}), bf16[2,4,256,128]{3,2,0,1:T(8,128)(2,1)S(1)}, u32[]{:S(2)}, u32[]{:S(2)}) async-start(bf16[2,4,256,128]{3,2,0,1:T(8,128)(2,1)} %pad_maximum_fusion), calls=%async_computation.1 | async-start | bytes 1048576 | tf_op jit(solution)/shard_map/all_to_all | solution.py:39
  80.1 8.5 %all-to-all-done.1 = bf16[2,4,256,128]{3,2,0,1:T(8,128)(2,1)S(1)} async-done(((bf16[2,4,256,128]{3,2,0,1:T(8,128)(2,1)}), bf16[2,4,256,128]{3,2,0,1:T(8,128)(2,1)S(1)}, u32[]{:S(2)}, u32[]{:S(2)}) %all-to-all-start.1) | async-done | bytes 524320 | tf_op jit(solution)/shard_map/all_to_all | solution.py:39
  88.6 1.9 %gather_fusion.1 = bf16[512,128]{1,0:T(8,128)(2,1)} fusion(bf16[1024,128]{1,0:T(8,128)(2,1)S(1)} %bitcast.32, s32[1024]{0:T(1024)S(1)} %pad_clamp_fusion), kind=kCustom, calls=%fused_computation.1 | custom fusion | bytes 264192 | tf_op jit(solution)/shard_map/gather | solution.py:42
  90.5 1.9 %gather_fusion = bf16[512,128]{1,0:T(8,128)(2,1)} fusion(bf16[1024,128]{1,0:T(8,128)(2,1)S(1)} %bitcast.31, s32[1024]{0:T(1024)S(1)} %pad_clamp_fusion), kind=kCustom, calls=%fused_computation | custom fusion | bytes 264192 | tf_op jit(solution)/shard_map/gather | solution.py:42
  (2 shorter events, 0.0 us)
Async XLA Ops:
  7.2 34.3 %all-gather.2.cloned.1.call-start = ((), (), s32[]{:S(2)}) async-start(), calls=%async_computation.2 | async-start | bytes 2359296 | tf_op jit(solution)/shard_map/all_gather | solution.py:31
  56.1 15.0 %copy-start = (bf16[8192,128]{1,0:T(8,128)(2,1)S(1)}, bf16[8192,128]{1,0:T(8,128)(2,1)}, u32[]{:S(2)}) copy-start(bf16[8192,128]{1,0:T(8,128)(2,1)} %all-gather.2.cloned.1.call-done) | copy-start | bytes 6291460
  76.4 12.1 %all-to-all-start.1 = ((bf16[2,4,256,128]{3,2,0,1:T(8,128)(2,1)}), bf16[2,4,256,128]{3,2,0,1:T(8,128)(2,1)S(1)}, u32[]{:S(2)}, u32[]{:S(2)}) async-start(bf16[2,4,256,128]{3,2,0,1:T(8,128)(2,1)} %pad_maximum_fusion), calls=%async_computation.1 | async-start | bytes 1048576 | tf_op jit(solution)/shard_map/all_to_all | solution.py:39
Sparse Core Ops, SparseCore 0:
  9.6 31.8 all-gather.1
where the time goes:
time: 99.7 us; the launch traced here: 99.3 us
  waiting for transfers between devices  26 us (26%)
  other arithmetic  21.6 us (22%)
  matrix products  19.1 us (19%)
  between operations  14.1 us (14%)
  blocking collectives  10.7 us (11%)
  local copies, waits for them, and re-layouts  4.08 us (4%)
  starting transfers between devices  3.69 us (4%)
    all_gather x1, waiting for transfers between devices, local(): piece = lax.all_gather(centroids, 'blk', axis=0, tiled=True)  16.8 us
    reduce_sum x1, other arithmetic, local(): total = jnp.sum(weights.astype(jnp.float32), axis=1)  15 us
    dot_general x1, matrix products, scores_of(): lax.dot_general(queries, piece, (((1,), (1,)), ((), ())), preferred_eleme...  14.6 us
    all_to_all x1, blocking collectives, local(): lax.all_to_all(outgoing.reshape(loops, cap, width), 'cell', split_axis=0,...  10.7 us
    all_to_all x1, waiting for transfers between devices, local(): lax.all_to_all(stacked, 'cell', split_axis=1, concat_axis=1, tiled=True)  8.47 us
    dot_general x1, matrix products, local(): numer = jnp.dot(weights, piece, preferred_element_type=jnp.float32)  4.49 us
    gather x2, local copies, waits for them, and re-layouts, local(): return (back[0][slots], back[1][slots])  3.83 us
    all_to_all x1, starting transfers between devices, local(): lax.all_to_all(stacked, 'cell', split_axis=1, concat_axis=1, tiled=True)  3.65 us
  transfers between devices with their start and end apart: 2, of which 2 were waited for; matrix products, arithmetic and copies ran while one was open for 6% of the time, Pallas kernels for 0%

commit v1 on v0

--- a/solution.py
+++ b/solution.py
@@ -3,6 +3,30 @@
 import jax.numpy as jnp
 from jax import lax
 from jax.sharding import PartitionSpec as P
+
+
+def cut_along(shard, dim, devices):
+    dims = shard.shape
+    blocks = shard.reshape(*dims[:dim], devices, dims[dim] // devices, *dims[dim + 1 :])
+    return jnp.moveaxis(blocks, dim, 0)
+
+
+def in_order(blocks, dim):
+    blocks = jnp.moveaxis(blocks, 0, dim)
+    lengths = blocks.shape
+    return blocks.reshape(*lengths[:dim], lengths[dim] * lengths[dim + 1], *lengths[dim + 2 :])
+
+
+def rotated_exchange(array, axis, split_dim, concat_dim):
+    devices, index = (lax.axis_size(axis), lax.axis_index(axis))
+    blocks = cut_along(array, split_dim, devices)
+    out = blocks
+    for step in range(1, devices):
+        target, source = ((index + step) % devices, (index - step) % devices)
+        sent = lax.dynamic_index_in_dim(blocks, target, 0)
+        other = lax.ppermute(sent, axis, [(i, (i + step) % devices) for i in range(devices)])
+        out = lax.dynamic_update_slice_in_dim(out, other, source, axis=0)
+    return in_order(out, concat_dim)
 
 
 def local(codes, scales, coarse_ids, centroids):
@@ -36,9 +60,7 @@
     recon = (numer / total[:, None]).astype(jnp.bfloat16)
     remote_residual = (queries.astype(jnp.float32) - recon.astype(jnp.float32)).astype(jnp.bfloat16)
     stacked = jnp.stack([recon, remote_residual]).reshape(2, loops, cap, width)
-    back = lax.all_to_all(stacked, "cell", split_axis=1, concat_axis=1, tiled=True).reshape(
-        2, loops * cap, width
-    )
+    back = rotated_exchange(stacked, "cell", 1, 1).reshape(2, loops * cap, width)
     return (back[0][slots], back[1][slots])
 
 

time: 99.7 us -> 96.2 us (0.965)
  blocking collectives: 10.7 us -> 0 us
  starting transfers between devices: 3.69 us -> 9.73 us
  waiting for transfers between devices: 26 us -> 27.3 us
    all_to_all x1 -> x0, blocking collectives: 10.7 us -> none  [local(): lax.all_to_all(outgoing.reshape(loops, cap, width), 'cell', split_axis=0,...]
    ppermute x0 -> x3, waiting for transfers between devices: none -> 4.82 us  [rotated_exchange(): lax.ppermute(sent, axis, [(i, (i + step) % devices) for i in range(device...]
    ppermute x0 -> x3, starting transfers between devices: none -> 4.51 us  [rotated_exchange(): lax.ppermute(sent, axis, [(i, (i + step) % devices) for i in range(device...]
    all_to_all x1, waiting for transfers between devices: 8.47 us -> 5.37 us  [local(): lax.all_to_all(outgoing.reshape(loops, cap, width), 'cell', split_axis=0,...]
    all_to_all x1, starting transfers between devices: 3.65 us -> 5.19 us  [local(): lax.all_to_all(outgoing.reshape(loops, cap, width), 'cell', split_axis=0,...]
    another operation x3 -> x2, other arithmetic: 2.22 us -> 1.39 us
  transfers between devices with their start and end apart: 2 -> 5, of which waited for: 2 -> 4; matrix products, arithmetic and copies ran while one was open for 6% -> 7% of each run, Pallas kernels for 0% -> 0%
where the time goes in v1:
time: 96.2 us; the launch traced here: 95.8 us
  waiting for transfers between devices  27.3 us (28%)
  other arithmetic  21.5 us (22%)
  matrix products  19.1 us (20%)
  between operations  14.1 us (15%)
  starting transfers between devices  9.73 us (10%)
  local copies, waits for them, and re-layouts  4.14 us (4%)
    all_gather x1, waiting for transfers between devices, local(): piece = lax.all_gather(centroids, 'blk', axis=0, tiled=True)  16.4 us
    reduce_sum x1, other arithmetic, local(): total = jnp.sum(weights.astype(jnp.float32), axis=1)  15 us
    dot_general x1, matrix products, scores_of(): lax.dot_general(queries, piece, (((1,), (1,)), ((), ())), preferred_eleme...  14.6 us
    all_to_all x1, waiting for transfers between devices, local(): lax.all_to_all(outgoing.reshape(loops, cap, width), 'cell', split_axis=0,...  5.37 us
    all_to_all x1, starting transfers between devices, local(): lax.all_to_all(outgoing.reshape(loops, cap, width), 'cell', split_axis=0,...  5.19 us
    ppermute x3, waiting for transfers between devices, rotated_exchange(): lax.ppermute(sent, axis, [(i, (i + step) % devices) for i in range(device...  4.82 us
    ppermute x3, starting transfers between devices, rotated_exchange(): lax.ppermute(sent, axis, [(i, (i + step) % devices) for i in range(device...  4.51 us
    dot_general x1, matrix products, local(): numer = jnp.dot(weights, piece, preferred_element_type=jnp.float32)  4.49 us
  transfers between devices with their start and end apart: 5, of which 4 were waited for; matrix products, arithmetic and copies ran while one was open for 7% of the time, Pallas kernels for 0%

profile of v1, /device:TPU:0, one launch (start us, length us, event | category | flops | bytes accessed | tf_op | source)
XLA Modules:
  0.0 95.8 jit_solution(1031271490931670138)
XLA Ops:
  7.2 0.0 all-gather.2.cloned.1.call-start
  7.2 0.7 all-gather.2.cloned.1.call-update
  7.9 0.7 fusion.13
  8.6 1.2 %reduce-window.6 = s32[4,4,128]{2,1,0:T(4,128)S(1)} reduce-window(s32[4,4,128]{2,1,0:T(4,128)S(1)} %fusion.13, s32[]{:T(128)} %constant.64.clone.1), window={size=1x1x128 pad=0_0x0_0x127_0}, to_apply=%region_0.0 | reduce-window | flops 260096 | bytes 16388 | tf_op jit(solution)/shard_map/reduce-window
  9.8 0.2 slice_reduce_fusion
  10.0 0.2 reduce-window.9
  10.2 0.1 add_bitcast_fusion
  10.3 0.7 fusion.12
  11.0 0.7 compare_select_fusion
  11.7 2.9 %scatter_custom_fusion = bf16[1024,128]{1,0:T(8,128)(2,1)} fusion(s32[512]{0:T(512)S(1)} %compare_select_fusion, bf16[512,128]{1,0:T(8,128)(2,1)} %param.4, f32[512]{0:T(512)} %param.5, bf16[]{:T(256)} %constant.62.clone.1), kind=kCustom, calls=%fused_computation.18 | custom fusion | flops 196608 | bytes 395266 | tf_op jit(solution)/shard_map/scatter | solution.py:42
  14.5 5.2 %all-to-all-start = ((bf16[4,256,128]{2,1,0:T(8,128)(2,1)}), bf16[4,256,128]{2,1,0:T(8,128)(2,1)S(1)}, u32[]{:S(2)}, u32[]{:S(2)}) async-start(bf16[4,256,128]{2,1,0:T(8,128)(2,1)} %bitcast.2), calls=%async_computation | async-start | bytes 524288 | tf_op jit(solution)/shard_map/all_to_all | solution.py:43
  19.7 5.4 %all-to-all-done = bf16[4,256,128]{2,1,0:T(8,128)(2,1)S(1)} async-done(((bf16[4,256,128]{2,1,0:T(8,128)(2,1)}), bf16[4,256,128]{2,1,0:T(8,128)(2,1)S(1)}, u32[]{:S(2)}, u32[]{:S(2)}) %all-to-all-start) | async-done | bytes 262176 | tf_op jit(solution)/shard_map/all_to_all | solution.py:43
  25.1 16.4 %all-gather.2.cloned.1.call-done = bf16[8192,128]{1,0:T(8,128)(2,1)} async-done(((bf16[1024,128]{1,0:T(8,128)(2,1)}), bf16[8192,128]{1,0:T(8,128)(2,1)}) %all-gather.2.cloned.1.call-update) | async-done | bytes 2097168 | tf_op jit(solution)/shard_map/all_gather | solution.py:55
  41.5 14.6 %multiply_reduce_fusion = (f32[1024]{0:T(1024)S(1)}, f32[1024,8192]{1,0:T(8,128)}) fusion(bf16[1024,128]{1,0:T(8,128)(2,1)S(1)} %bitcast.39, bf16[8192,128]{1,0:T(8,128)(2,1)} %all-gather.2.cloned.1.call-done), kind=kOutput, calls=%fused_computation.5 | convolution fusion | flops 2164259840 | bytes 35917824 | tf_op jit(solution)/shard_map/dot_general | solution.py:49
  56.1 15.0 %convert_reduce_fusion = (f32[1024]{0:T(1024)S(1)}, bf16[1024,8192]{1,0:T(8,128)(2,1)S(1)}) fusion(f32[1024]{0:T(1024)S(1)} %get-tuple-element.9, f32[1024,8192]{1,0:T(8,128)} %get-tuple-element.10), kind=kLoop, calls=%fused_computation.3 | loop fusion | flops 41942016 | bytes 50339840 | tf_op jit(solution)/shard_map/reduce_sum | solution.py:57
  71.1 4.5 %subtract_convert_fusion = (bf16[1024,128]{1,0:T(8,128)(2,1)S(1)}, bf16[1024,128]{1,0:T(8,128)(2,1)S(1)}) fusion(bf16[4,256,128]{2,1,0:T(8,128)(2,1)S(1)} %all-to-all-done, f32[1024]{0:T(1024)S(1)} %get-tuple-element.2, bf16[1024,8192]{1,0:T(8,128)(2,1)S(1)} %get-tuple-element.3, bf16[8192,128]{1,0:T(8,128)(2,1)S(1)} %copy-done), kind=kOutput, calls=%fused_computation.16 | convolution fusion | flops 2148270080 | bytes 19664896 | tf_op jit(solution)/shard_map/dot_general | solution.py:58
  75.6 1.5 %collective-permute-start = (bf16[1,2,1,256,128]{4,3,0,2,1:T(8,128)(2,1)S(1)}, bf16[1,2,1,256,128]{4,3,0,2,1:T(8,128)(2,1)S(1)}, u32[]{:S(2)}, u32[]{:S(2)}) collective-permute-start(bf16[1,2,1,256,128]{4,3,0,2,1:T(8,128)(2,1)S(1)} %get-tuple-element.7), channel_id=1, source_target_pairs={{0,8},{8,16},{16,24},{24,0},{1,9},{9,17},{17,25},{25,1},{2,10},{10... | collective-permute-start | bytes 393224 | tf_op jit(solution)/shard_map/ppermute | solution.py:27
  77.2 1.5 %collective-permute-start.1 = (bf16[1,2,1,256,128]{4,3,0,2,1:T(8,128)(2,1)S(1)}, bf16[1,2,1,256,128]{4,3,0,2,1:T(8,128)(2,1)S(1)}, u32[]{:S(2)}, u32[]{:S(2)}) collective-permute-start(bf16[1,2,1,256,128]{4,3,0,2,1:T(8,128)(2,1)S(1)} %get-tuple-element.8), channel_id=1, source_target_pairs={{0,16},{8,24},{16,0},{24,8},{1,17},{9,25},{17,1},{25,9},{2,18},{10... | collective-permute-start | bytes 393224 | tf_op jit(solution)/shard_map/ppermute | solution.py:27
  78.6 0.1 fusion.1
  78.7 1.5 %collective-permute-start.2 = (bf16[1,2,1,256,128]{4,3,0,2,1:T(8,128)(2,1)S(1)}, bf16[1,2,1,256,128]{4,3,0,2,1:T(8,128)(2,1)S(1)}, u32[]{:S(2)}, u32[]{:S(2)}) collective-permute-start(bf16[1,2,1,256,128]{4,3,0,2,1:T(8,128)(2,1)S(1)} %get-tuple-element.6), channel_id=1, source_target_pairs={{0,24},{8,0},{16,8},{24,16},{1,25},{9,1},{17,9},{25,17},{2,26},{10... | collective-permute-start | bytes 393224 | tf_op jit(solution)/shard_map/ppermute | solution.py:27
  80.2 2.8 %collective-permute-done = bf16[1,2,1,256,128]{4,3,0,2,1:T(8,128)(2,1)S(1)} collective-permute-done((bf16[1,2,1,256,128]{4,3,0,2,1:T(8,128)(2,1)S(1)}, bf16[1,2,1,256,128]{4,3,0,2,1:T(8,128)(2,1)S(1)}, u32[]{:S(2)}, u32[]{:S(2)}) %collective-permute-start) | collective-permute-done | bytes 131104 | tf_op jit(solution)/shard_map/ppermute | solution.py:27
  83.0 2.0 %collective-permute-done.1 = bf16[1,2,1,256,128]{4,3,0,2,1:T(8,128)(2,1)S(1)} collective-permute-done((bf16[1,2,1,256,128]{4,3,0,2,1:T(8,128)(2,1)S(1)}, bf16[1,2,1,256,128]{4,3,0,2,1:T(8,128)(2,1)S(1)}, u32[]{:S(2)}, u32[]{:S(2)}) %collective-permute-start.1) | collective-permute-done | bytes 131104 | tf_op jit(solution)/shard_map/ppermute | solution.py:27
  85.1 1.9 %gather_fusion = bf16[512,128]{1,0:T(8,128)(2,1)} fusion(bf16[1024,128]{1,0:T(8,128)(2,1)S(1)} %bitcast.37, s32[1024]{0:T(1024)S(1)} %pad_clamp_fusion), kind=kCustom, calls=%fused_computation | custom fusion | bytes 264192 | tf_op jit(solution)/shard_map/gather | solution.py:64
  87.1 1.9 %gather_fusion.1 = bf16[512,128]{1,0:T(8,128)(2,1)} fusion(bf16[1024,128]{1,0:T(8,128)(2,1)S(1)} %bitcast.36, s32[1024]{0:T(1024)S(1)} %pad_clamp_fusion), kind=kCustom, calls=%fused_computation.1 | custom fusion | bytes 264192 | tf_op jit(solution)/shard_map/gather | solution.py:64
  (9 shorter events, 0.2 us)
Async XLA Ops:
  7.2 34.3 %all-gather.2.cloned.1.call-start = ((), (), s32[]{:S(2)}) async-start(), calls=%async_computation.1 | async-start | bytes 2359296 | tf_op jit(solution)/shard_map/all_gather | solution.py:55
  14.5 10.6 %all-to-all-start = ((bf16[4,256,128]{2,1,0:T(8,128)(2,1)}), bf16[4,256,128]{2,1,0:T(8,128)(2,1)S(1)}, u32[]{:S(2)}, u32[]{:S(2)}) async-start(bf16[4,256,128]{2,1,0:T(8,128)(2,1)} %bitcast.2), calls=%async_computation | async-start | bytes 524288 | tf_op jit(solution)/shard_map/all_to_all | solution.py:43
  56.1 15.0 %copy-start = (bf16[8192,128]{1,0:T(8,128)(2,1)S(1)}, bf16[8192,128]{1,0:T(8,128)(2,1)}, u32[]{:S(2)}) copy-start(bf16[8192,128]{1,0:T(8,128)(2,1)} %all-gather.2.cloned.1.call-done) | copy-start | bytes 6291460
  75.6 7.4 %collective-permute-start = (bf16[1,2,1,256,128]{4,3,0,2,1:T(8,128)(2,1)S(1)}, bf16[1,2,1,256,128]{4,3,0,2,1:T(8,128)(2,1)S(1)}, u32[]{:S(2)}, u32[]{:S(2)}) collective-permute-start(bf16[1,2,1,256,128]{4,3,0,2,1:T(8,128)(2,1)S(1)} %get-tuple-element.7), channel_id=1, source_target_pairs={{0,8},{8,16},{16,24},{24,0},{1,9},{9,17},{17,25},{25,1},{2,10},{10... | collective-permute-start | bytes 393224 | tf_op jit(solution)/shard_map/ppermute | solution.py:27
  77.2 7.9 %collective-permute-start.1 = (bf16[1,2,1,256,128]{4,3,0,2,1:T(8,128)(2,1)S(1)}, bf16[1,2,1,256,128]{4,3,0,2,1:T(8,128)(2,1)S(1)}, u32[]{:S(2)}, u32[]{:S(2)}) collective-permute-start(bf16[1,2,1,256,128]{4,3,0,2,1:T(8,128)(2,1)S(1)} %get-tuple-element.8), channel_id=1, source_target_pairs={{0,16},{8,24},{16,0},{24,8},{1,17},{9,25},{17,1},{25,9},{2,18},{10... | collective-permute-start | bytes 393224 | tf_op jit(solution)/shard_map/ppermute | solution.py:27
  78.7 6.4 %collective-permute-start.2 = (bf16[1,2,1,256,128]{4,3,0,2,1:T(8,128)(2,1)S(1)}, bf16[1,2,1,256,128]{4,3,0,2,1:T(8,128)(2,1)S(1)}, u32[]{:S(2)}, u32[]{:S(2)}) collective-permute-start(bf16[1,2,1,256,128]{4,3,0,2,1:T(8,128)(2,1)S(1)} %get-tuple-element.6), channel_id=1, source_target_pairs={{0,24},{8,0},{16,8},{24,16},{1,25},{9,1},{17,9},{25,17},{2,26},{10... | collective-permute-start | bytes 393224 | tf_op jit(solution)/shard_map/ppermute | solution.py:27
Sparse Core Ops, SparseCore 0:
  9.6 31.8 all-gather.1
